TPU v7x, 32 devices: a whole 2x2x4 slice. The times are simulated.
32 devices in a mesh: grp: 2 (over x), blade: 8 (over z, y), dof: 2 (over core).
Axes of the slice: x: 2, y: 2, z: 4, core: 2. Of those that a mesh axis runs over, the one named last changes fastest.
Arguments:
- panel: bfloat16 [8192, 512], P(('grp', 'blade', 'dof')), parts along dimension 0, may hold values from -0.25 to 0.25
- stiffness: bfloat16 [96, 64, 128, 128], P(('grp', 'blade'), 'dof'), parts along dimension 0, may hold values from -0.5 to 0.5
- block_rows: int32 [96, 64], P(('grp', 'blade'), 'dof'), parts along dimension 0, may hold values from 0 to 31
- block_cols: int32 [96, 64], P(('grp', 'blade'), 'dof'), parts along dimension 0, may hold values from 0 to 31
Outputs:
- spectral: float32 [2, 96, 512, 512], P(None, ('grp', 'blade'), 'dof'), parts along dimension 1
There are 2 independent parts, one for each index of `grp`. A program takes and returns all parts, laid end to end along the dimension named above; each array names one. Nothing has to cross between parts.
Inputs may be any that keep to these rules, and one draw needn't show every extreme that they name: `block_rows`: row block index of each stiffness block; indices of one blade may repeat. `block_cols`: column block index of each stiffness block; indices of one blade may repeat.
All inputs are finite; a program needn't handle non-finite values.
Results may differ from a plain program's by a relative error of at most 0.0029.
Values may be sent and summed in bfloat16 or wider, within the bound.
No kernel may reach another device: no remote copies, remote signals or barrier semaphores. Data moves between devices by JAX's collectives and lax.ppermute only.
A program may use at most 128 MiB of HBM per device.

v0:
```python
import math
import jax
import jax.numpy as jnp
from jax import lax
from jax.sharding import PartitionSpec as P


def body(panel, stiffness, block_rows, block_cols):
    block_size = stiffness.shape[-1]
    modes = panel.shape[-1]
    whole = lax.all_gather(panel, ("blade", "dof"), axis=0, tiled=True)
    blocks = whole.reshape(-1, block_size, modes)

    def one_blade(items):
        mats, rows, cols = items
        chosen = jnp.take(blocks, cols, axis=0)
        image = jnp.einsum("nij,njm->nim", mats, chosen, preferred_element_type=jnp.float32)
        image = image.astype(jnp.bfloat16)
        left = jnp.take(blocks, rows, axis=0).reshape(-1, modes)
        return lax.dot_general(
            left,
            image.reshape(-1, modes),
            (((0,), (0,)), ((), ())),
            preferred_element_type=jnp.float32,
        )

    partial_proj = lax.map(one_blade, (stiffness, block_rows, block_cols))
    blade_count = stiffness.shape[0] * lax.axis_size("blade")
    index = jnp.arange(blade_count, dtype=jnp.int32)
    angle = (index[:, None] * index[None, :] % blade_count).astype(jnp.float32) * (
        2.0 * math.pi / blade_count
    )
    cosine = jnp.cos(angle)
    sine = jnp.sin(angle)
    stacked = lax.all_to_all(partial_proj, "blade", split_axis=1, concat_axis=0, tiled=True)
    real_part = jnp.einsum("hb,brc->hrc", cosine, stacked, precision=lax.Precision.HIGHEST)
    imag_part = -jnp.einsum("hb,brc->hrc", sine, stacked, precision=lax.Precision.HIGHEST)
    joined = jnp.stack([real_part, imag_part])
    full_spec = lax.all_to_all(joined, "blade", split_axis=1, concat_axis=2, tiled=True)
    result = lax.psum_scatter(full_spec, "dof", scatter_dimension=2, tiled=True)
    return result


def solution(mesh):
    placed = (
        P(("grp", "blade", "dof"), None),
        P(("grp", "blade"), "dof", None, None),
        P(("grp", "blade"), "dof"),
        P(("grp", "blade"), "dof"),
    )
    return jax.shard_map(
        body,
        mesh=mesh,
        in_specs=placed,
        out_specs=P(None, ("grp", "blade"), "dof", None),
        check_vma=False,
    )
```

profile of v0, /device:TPU:0, one launch (start us, length us, event | category | flops | bytes accessed | tf_op | source)
XLA Modules:
  0.0 863.4 jit_solution(7075036304253567163)
XLA Ops:
  7.3 55.5 %all-gather.2.cloned.1.call-done = bf16[4096,512]{1,0:T(8,128)(2,1)} async-done(((bf16[256,512]{1,0:T(8,128)(2,1)}), bf16[4096,512]{1,0:T(8,128)(2,1)}) %all-gather.2.cloned.1.call-update) | async-done | bytes 4194320 | tf_op jit(solution)/shard_map/all_gather | solution.py:11
  62.8 244.8 %while.10 = (s32[]{:T(128)}, f32[6,512,512]{2,0,1:T(8,128)}, s32[6,32]{1,0:T(8,128)}, bf16[32,128,512]{2,1,0:T(8,128)(2,1)}, bf16[6,32,128,128]{3,2,1,0:T(8,128)...) while((s32[]{:T(128)}, f32[6,512,512]{2,0,1:T(8,128)}, s32[6,32]{1,0:T(8,128)}, ...), condition=%wide.region_1.3_spmd, body=%wide.region_0.2_spmd.sunk | while | flops 2690648576 | bytes 31466728 | solution.py:27
  63.5 4.9 gather_fusion.1
  68.5 5.0 gather_fusion
  73.5 7.2 fusion.71
  81.8 21.8 %dynamic_update_slice.5 = f32[6,512,512]{2,0,1:T(8,128)} dynamic-update-slice(f32[6,512,512]{2,0,1:T(8,128)} %get-tuple-element.111, f32[1,512,512]{2,0,1:T(1,128)S(1)} %copy.41, s32[]{:T(128)S(6)} %copy.45, s32[]{:T(128)} %constant.36.clone.1..sunk, s32[]{:T(128)} %constant.36.clone.1..sunk) | dynamic-update-slice | bytes 2097156 | tf_op jit(solution)/shard_map/while/body/jit(dynamic_update_index_in_dim)/dynamic_update_slice | solution.py:27
  104.3 4.9 gather_fusion.1
  109.3 5.0 gather_fusion
  114.3 7.2 fusion.71
  122.6 21.8 %dynamic_update_slice.5 = f32[6,512,512]{2,0,1:T(8,128)} dynamic-update-slice(f32[6,512,512]{2,0,1:T(8,128)} %get-tuple-element.111, f32[1,512,512]{2,0,1:T(1,128)S(1)} %copy.41, s32[]{:T(128)S(6)} %copy.45, s32[]{:T(128)} %constant.36.clone.1..sunk, s32[]{:T(128)} %constant.36.clone.1..sunk) | dynamic-update-slice | bytes 2097156 | tf_op jit(solution)/shard_map/while/body/jit(dynamic_update_index_in_dim)/dynamic_update_slice | solution.py:27
  145.1 4.9 gather_fusion.1
  150.1 5.0 gather_fusion
  155.1 7.2 fusion.71
  163.4 21.8 %dynamic_update_slice.5 = f32[6,512,512]{2,0,1:T(8,128)} dynamic-update-slice(f32[6,512,512]{2,0,1:T(8,128)} %get-tuple-element.111, f32[1,512,512]{2,0,1:T(1,128)S(1)} %copy.41, s32[]{:T(128)S(6)} %copy.45, s32[]{:T(128)} %constant.36.clone.1..sunk, s32[]{:T(128)} %constant.36.clone.1..sunk) | dynamic-update-slice | bytes 2097156 | tf_op jit(solution)/shard_map/while/body/jit(dynamic_update_index_in_dim)/dynamic_update_slice | solution.py:27
  185.9 4.9 gather_fusion.1
  190.9 5.0 gather_fusion
  195.9 7.2 fusion.71
  204.2 21.8 %dynamic_update_slice.5 = f32[6,512,512]{2,0,1:T(8,128)} dynamic-update-slice(f32[6,512,512]{2,0,1:T(8,128)} %get-tuple-element.111, f32[1,512,512]{2,0,1:T(1,128)S(1)} %copy.41, s32[]{:T(128)S(6)} %copy.45, s32[]{:T(128)} %constant.36.clone.1..sunk, s32[]{:T(128)} %constant.36.clone.1..sunk) | dynamic-update-slice | bytes 2097156 | tf_op jit(solution)/shard_map/while/body/jit(dynamic_update_index_in_dim)/dynamic_update_slice | solution.py:27
  231.7 5.0 gather_fusion
  236.7 7.2 fusion.71
  245.0 21.8 %dynamic_update_slice.5 = f32[6,512,512]{2,0,1:T(8,128)} dynamic-update-slice(f32[6,512,512]{2,0,1:T(8,128)} %get-tuple-element.111, f32[1,512,512]{2,0,1:T(1,128)S(1)} %copy.41, s32[]{:T(128)S(6)} %copy.45, s32[]{:T(128)} %constant.36.clone.1..sunk, s32[]{:T(128)} %constant.36.clone.1..sunk) | dynamic-update-slice | bytes 2097156 | tf_op jit(solution)/shard_map/while/body/jit(dynamic_update_index_in_dim)/dynamic_update_slice | solution.py:27
  272.5 5.0 gather_fusion
  277.5 7.2 fusion.71
  285.8 21.8 %dynamic_update_slice.5 = f32[6,512,512]{2,0,1:T(8,128)} dynamic-update-slice(f32[6,512,512]{2,0,1:T(8,128)} %get-tuple-element.111, f32[1,512,512]{2,0,1:T(1,128)S(1)} %copy.41, s32[]{:T(128)S(6)} %copy.45, s32[]{:T(128)} %constant.36.clone.1..sunk, s32[]{:T(128)} %constant.36.clone.1..sunk) | dynamic-update-slice | bytes 2097156 | tf_op jit(solution)/shard_map/while/body/jit(dynamic_update_index_in_dim)/dynamic_update_slice | solution.py:27
  307.6 187.5 %all_to_all.36 = f32[6,512,512]{2,0,1:T(8,128)S(1)} all-to-all(f32[6,512,512]{2,0,1:T(8,128)} %get-tuple-element.38), channel_id=1, replica_groups=mesh['grp'=2,'blade'=8,'dof'=2] {'blade'}, dimensions={1} | all-to-all | bytes 12582912 | tf_op jit(solution)/shard_map/all_to_all | solution.py:35
  498.6 9.7 %negate_bitcast_fusion = f32[1,48,64,512]{3,1,2,0:T(8,128)S(1)} fusion(f32[48,64,512]{2,1,0:T(8,128)S(1)} %bitcast.41), kind=kOutput, calls=%fused_computation.26 | convolution fusion | flops 907563264 | bytes 12582912 | tf_op jit(solution)/shard_map/hb,brc->hrc/dot_general | solution.py:37
  508.3 10.2 %fusion.34 = f32[1,48,64,512]{3,1,2,0:T(8,128)} fusion(f32[48,64,512]{2,1,0:T(8,128)S(1)} %bitcast.42), kind=kOutput, calls=%fused_computation.31 | convolution fusion | flops 905990400 | bytes 12582912 | tf_op jit(solution)/shard_map/hb,brc->hrc/dot_general | solution.py:36
  518.5 9.5 %pad_maximum_fusion = f32[2,48,64,512]{3,1,2,0:T(8,128)} fusion(f32[1,48,64,512]{3,1,2,0:T(8,128)S(1)} %negate_bitcast_fusion, f32[1,48,64,512]{3,1,2,0:T(8,128)} %fusion.34), kind=kLoop, calls=%fused_computation.25 | loop fusion | flops 3145728 | bytes 25165824 | tf_op jit(solution)/shard_map/stack | solution.py:38
  528.0 16.4 %copy.24 = f32[2,48,64,512]{3,2,0,1:T(8,128)} copy(f32[2,48,64,512]{3,1,2,0:T(8,128)} %pad_maximum_fusion) | data formatting | bytes 25165824 | tf_op jit(solution)/shard_map/stack | solution.py:38
  544.4 279.6 %all_to_all.37 = f32[2,48,64,512]{3,2,0,1:T(8,128)} all-to-all(f32[2,48,64,512]{3,2,0,1:T(8,128)} %copy.24), channel_id=1, replica_groups=mesh['grp'=2,'blade'=8,'dof'=2] {'blade'}, dimensions={1} | all-to-all | bytes 25165824 | tf_op jit(solution)/shard_map/all_to_all | solution.py:39
  823.9 12.0 %copy.26 = f32[2,6,8,64,512]{4,3,2,1,0:T(8,128)} copy(f32[2,6,8,64,512]{4,3,0,1,2:T(8,128)} %bitcast.44) | data formatting | bytes 25165824 | tf_op jit(solution)/shard_map/all_to_all | solution.py:39
  835.9 20.6 %reduce-scatter.2.cloned.1.call-done = f32[2,6,256,512]{3,2,1,0:T(8,128)} async-done(((f32[2,6,512,512]{3,2,1,0:T(8,128)}), f32[2,6,256,512]{3,2,1,0:T(8,128)}) %reduce-scatter.2.cloned.1.call-update) | async-done | bytes 6291472 | tf_op jit(solution)/shard_map/reduce_scatter | solution.py:40
  (32 shorter events, 25.0 us)
Async XLA Ops:
  6.5 56.3 %all-gather.2.cloned.1.call-start = ((), (), s32[]{:S(2)}) async-start(), calls=%async_computation.3 | async-start | bytes 4456448 | tf_op jit(solution)/shard_map/all_gather | solution.py:11
  7.3 849.3 %reduce-scatter.2.cloned.1.call-start = ((), (), s32[]{:S(2)}) async-start(), calls=%async_computation.4 | async-start | bytes 18874368 | tf_op jit(solution)/shard_map/reduce_scatter | solution.py:40
Sparse Core Ops, SparseCore 0:
  9.5 53.2 all-gather.1
  836.0 20.4 reduce-scatter.1
where the time goes:
time: 868 us; the launch traced here: 863 us
  blocking collectives  467 us (54%)
  local copies, waits for them, and re-layouts  229 us (26%)
  waiting for transfers between devices  76.9 us (9%)
  matrix products  63.3 us (7%)
  other arithmetic  13.8 us (2%)
  between operations  13.4 us (2%)
    all_to_all x1, blocking collectives, body(): lax.all_to_all(joined, 'blade', split_axis=1, concat_axis=2, tiled=True)  280 us
    all_to_all x1, blocking collectives, body(): lax.all_to_all(partial_proj, 'blade', split_axis=1, concat_axis=0, tiled=...  187 us
    dynamic_update_slice x12, local copies, waits for them, and re-layouts, body(): partial_proj = lax.map(one_blade, (stiffness, block_rows, block_cols))  137 us
    all_gather x1, waiting for transfers between devices, body(): whole = lax.all_gather(panel, ('blade', 'dof'), axis=0, tiled=True)  55.5 us
    dot_general x6, matrix products, one_blade(): lax.dot_general(left, image.reshape(-1, modes), (((0,), (0,)), ((), ())),...  43.5 us
    gather x6, local copies, waits for them, and re-layouts, one_blade(): chosen = jnp.take(blocks, cols, axis=0)  30.1 us
    gather x6, local copies, waits for them, and re-layouts, one_blade(): left = jnp.take(blocks, rows, axis=0).reshape(-1, modes)  29.7 us
    reduce_scatter x1, waiting for transfers between devices, body(): result = lax.psum_scatter(full_spec, 'dof', scatter_dimension=2, tiled=True)  20.6 us
  transfers between devices with their start and end apart: 2, of which 2 were waited for; matrix products, arithmetic and copies ran while one was open for 0% of the time, Pallas kernels for 0%

commit v1 on v0

--- a/solution.py
+++ b/solution.py
@@ -5,10 +5,31 @@
 from jax.sharding import PartitionSpec as P
 
 
+def ring_gather(shard, axis, dim):
+    peers, index, rows = (lax.axis_size(axis), lax.axis_index(axis), shard.shape[dim])
+    right = [(i, (i + 1) % peers) for i in range(peers)]
+    left = [(i, (i - 1) % peers) for i in range(peers)]
+    out = jnp.zeros((*shard.shape[:dim], peers * rows, *shard.shape[dim + 1 :]), shard.dtype)
+    out = lax.dynamic_update_slice_in_dim(out, shard, index * rows, axis=dim)
+    from_left = from_right = shard
+    middle = peers // 2
+    for hop in range(1, middle + 1):
+        from_left = lax.ppermute(from_left, axis, right)
+        out = lax.dynamic_update_slice_in_dim(
+            out, from_left, (index - hop) % peers * rows, axis=dim
+        )
+        if hop < peers - middle:
+            from_right = lax.ppermute(from_right, axis, left)
+            out = lax.dynamic_update_slice_in_dim(
+                out, from_right, (index + hop) % peers * rows, axis=dim
+            )
+    return out
+
+
 def body(panel, stiffness, block_rows, block_cols):
     block_size = stiffness.shape[-1]
     modes = panel.shape[-1]
-    whole = lax.all_gather(panel, ("blade", "dof"), axis=0, tiled=True)
+    whole = ring_gather(panel, ("blade", "dof"), 0)
     blocks = whole.reshape(-1, block_size, modes)
 
     def one_blade(items):

time: 868 us -> 895 us (1.031)
  starting transfers between devices: 0.04 us -> 32.9 us
  waiting for transfers between devices: 76.9 us -> 45.3 us
  local copies, waits for them, and re-layouts: 229 us -> 242 us
  matrix products: 63.3 us -> 74.2 us
    all_gather x1 -> x0, waiting for transfers between devices: 55.5 us -> none  [body(): whole = lax.all_gather(panel, ('blade', 'dof'), axis=0, tiled=True)]
    ppermute x0 -> x15, starting transfers between devices: none -> 32.9 us  [the longest x7 32.4 us: ring_gather(): from_right = lax.ppermute(from_right, axis, left)]
    ppermute x0 -> x15, waiting for transfers between devices: none -> 24.3 us  [the longest x8 17.5 us: ring_gather(): from_left = lax.ppermute(from_left, axis, right)]
    dynamic_update_slice x0 -> x16, local copies, waits for them, and re-layouts: none -> 11.5 us  [the longest x8 5.75 us: ring_gather(): lax.dynamic_update_slice_in_dim(out, from_left, (index - hop) % peers * r...]
    dot_general x1, matrix products: 9.7 us -> 20.6 us  [body(): jnp.einsum('hb,brc->hrc', sine, stacked, precision=lax.Precision.HIGHEST)]
  transfers between devices with their start and end apart: 2 -> 16, of which waited for: 2 -> 9; matrix products, arithmetic and copies ran while one was open for 0% -> 1% of each run, Pallas kernels for 0% -> 0%
where the time goes in v1:
time: 895 us; the launch traced here: 884 us
  blocking collectives  463 us (52%)
  local copies, waits for them, and re-layouts  242 us (27%)
  matrix products  74.2 us (8%)
  waiting for transfers between devices  45.3 us (5%)
  starting transfers between devices  32.9 us (4%)
  other arithmetic  13.8 us (2%)
  between operations  13.4 us (1%)
    all_to_all x1, blocking collectives, body(): lax.all_to_all(joined, 'blade', split_axis=1, concat_axis=2, tiled=True)  278 us
    all_to_all x1, blocking collectives, body(): lax.all_to_all(partial_proj, 'blade', split_axis=1, concat_axis=0, tiled=...  185 us
    dynamic_update_slice x12, local copies, waits for them, and re-layouts, body(): partial_proj = lax.map(one_blade, (stiffness, block_rows, block_cols))  137 us
    dot_general x6, matrix products, one_blade(): lax.dot_general(left, image.reshape(-1, modes), (((0,), (0,)), ((), ())),...  43.5 us
    ppermute x7, starting transfers between devices, ring_gather(): from_right = lax.ppermute(from_right, axis, left)  32.4 us
    gather x6, local copies, waits for them, and re-layouts, one_blade(): chosen = jnp.take(blocks, cols, axis=0)  29.8 us
    gather x6, local copies, waits for them, and re-layouts, one_blade(): left = jnp.take(blocks, rows, axis=0).reshape(-1, modes)  29.6 us
    reduce_scatter x1, waiting for transfers between devices, body(): result = lax.psum_scatter(full_spec, 'dof', scatter_dimension=2, tiled=True)  20.9 us
  transfers between devices with their start and end apart: 16, of which 9 were waited for; matrix products, arithmetic and copies ran while one was open for 1% of the time, Pallas kernels for 0%

profile of v1, /device:TPU:0, one launch (start us, length us, event | category | flops | bytes accessed | tf_op | source)
XLA Modules:
  0.0 884.4 jit_solution(2536369516847637638)
XLA Ops:
  7.0 5.0 collective-permute-start.1
  77.5 244.1 %while.10 = (s32[]{:T(128)}, f32[6,512,512]{2,0,1:T(8,128)}, s32[6,32]{1,0:T(8,128)}, bf16[32,128,512]{2,1,0:T(8,128)(2,1)}, bf16[6,32,128,128]{3,2,1,0:T(8,128)...) while((s32[]{:T(128)}, f32[6,512,512]{2,0,1:T(8,128)}, s32[6,32]{1,0:T(8,128)}, ...), condition=%wide.region_1.3_spmd, body=%wide.region_0.2_spmd.sunk | while | flops 2690648576 | bytes 31466728 | solution.py:48
  78.3 4.9 gather_fusion.1
  83.2 5.0 gather_fusion
  88.2 7.2 fusion.71
  96.5 21.7 %dynamic_update_slice.85 = f32[6,512,512]{2,0,1:T(8,128)} dynamic-update-slice(f32[6,512,512]{2,0,1:T(8,128)} %get-tuple-element.111, f32[1,512,512]{2,0,1:T(1,128)S(1)} %copy.41, s32[]{:T(128)S(6)} %copy.61, s32[]{:T(128)} %constant.127.clone.1..sunk, s32[]{:T(128)} %constant.127.clone.1..sunk) | dynamic-update-slice | bytes 2097156 | tf_op jit(solution)/shard_map/while/body/jit(dynamic_update_index_in_dim)/dynamic_update_slice | solution.py:48
  119.0 4.9 gather_fusion.1
  123.9 5.0 gather_fusion
  128.9 7.2 fusion.71
  137.2 21.7 %dynamic_update_slice.85 = f32[6,512,512]{2,0,1:T(8,128)} dynamic-update-slice(f32[6,512,512]{2,0,1:T(8,128)} %get-tuple-element.111, f32[1,512,512]{2,0,1:T(1,128)S(1)} %copy.41, s32[]{:T(128)S(6)} %copy.61, s32[]{:T(128)} %constant.127.clone.1..sunk, s32[]{:T(128)} %constant.127.clone.1..sunk) | dynamic-update-slice | bytes 2097156 | tf_op jit(solution)/shard_map/while/body/jit(dynamic_update_index_in_dim)/dynamic_update_slice | solution.py:48
  159.6 4.9 gather_fusion.1
  164.6 5.0 gather_fusion
  169.5 7.2 fusion.71
  177.9 21.7 %dynamic_update_slice.85 = f32[6,512,512]{2,0,1:T(8,128)} dynamic-update-slice(f32[6,512,512]{2,0,1:T(8,128)} %get-tuple-element.111, f32[1,512,512]{2,0,1:T(1,128)S(1)} %copy.41, s32[]{:T(128)S(6)} %copy.61, s32[]{:T(128)} %constant.127.clone.1..sunk, s32[]{:T(128)} %constant.127.clone.1..sunk) | dynamic-update-slice | bytes 2097156 | tf_op jit(solution)/shard_map/while/body/jit(dynamic_update_index_in_dim)/dynamic_update_slice | solution.py:48
  200.3 4.9 gather_fusion.1
  205.2 5.0 gather_fusion
  210.2 7.2 fusion.71
  218.5 21.7 %dynamic_update_slice.85 = f32[6,512,512]{2,0,1:T(8,128)} dynamic-update-slice(f32[6,512,512]{2,0,1:T(8,128)} %get-tuple-element.111, f32[1,512,512]{2,0,1:T(1,128)S(1)} %copy.41, s32[]{:T(128)S(6)} %copy.61, s32[]{:T(128)} %constant.127.clone.1..sunk, s32[]{:T(128)} %constant.127.clone.1..sunk) | dynamic-update-slice | bytes 2097156 | tf_op jit(solution)/shard_map/while/body/jit(dynamic_update_index_in_dim)/dynamic_update_slice | solution.py:48
  245.9 5.0 gather_fusion
  250.9 7.2 fusion.71
  259.2 21.7 %dynamic_update_slice.85 = f32[6,512,512]{2,0,1:T(8,128)} dynamic-update-slice(f32[6,512,512]{2,0,1:T(8,128)} %get-tuple-element.111, f32[1,512,512]{2,0,1:T(1,128)S(1)} %copy.41, s32[]{:T(128)S(6)} %copy.61, s32[]{:T(128)} %constant.127.clone.1..sunk, s32[]{:T(128)} %constant.127.clone.1..sunk) | dynamic-update-slice | bytes 2097156 | tf_op jit(solution)/shard_map/while/body/jit(dynamic_update_index_in_dim)/dynamic_update_slice | solution.py:48
  286.6 5.0 gather_fusion
  291.6 7.2 fusion.71
  299.9 21.7 %dynamic_update_slice.85 = f32[6,512,512]{2,0,1:T(8,128)} dynamic-update-slice(f32[6,512,512]{2,0,1:T(8,128)} %get-tuple-element.111, f32[1,512,512]{2,0,1:T(1,128)S(1)} %copy.41, s32[]{:T(128)S(6)} %copy.61, s32[]{:T(128)} %constant.127.clone.1..sunk, s32[]{:T(128)} %constant.127.clone.1..sunk) | dynamic-update-slice | bytes 2097156 | tf_op jit(solution)/shard_map/while/body/jit(dynamic_update_index_in_dim)/dynamic_update_slice | solution.py:48
  321.6 184.9 %all_to_all.36 = f32[6,512,512]{2,0,1:T(8,128)S(1)} all-to-all(f32[6,512,512]{2,0,1:T(8,128)} %get-tuple-element.38), channel_id=1, replica_groups=mesh['grp'=2,'blade'=8,'dof'=2] {'blade'}, dimensions={1} | all-to-all | bytes 12582912 | tf_op jit(solution)/shard_map/all_to_all | solution.py:56
  510.0 20.6 %negate_bitcast_fusion = f32[1,48,64,512]{3,1,2,0:T(8,128)S(1)} fusion(f32[48,64,512]{2,1,0:T(8,128)S(1)} %bitcast.40), kind=kOutput, calls=%fused_computation.26 | convolution fusion | flops 907563264 | bytes 12582912 | tf_op jit(solution)/shard_map/hb,brc->hrc/dot_general | solution.py:58
  530.6 10.2 %fusion.34 = f32[1,48,64,512]{3,1,2,0:T(8,128)} fusion(f32[48,64,512]{2,1,0:T(8,128)S(1)} %bitcast.41), kind=kOutput, calls=%fused_computation.31 | convolution fusion | flops 905990400 | bytes 12582912 | tf_op jit(solution)/shard_map/hb,brc->hrc/dot_general | solution.py:57
  540.8 9.5 %pad_maximum_fusion = f32[2,48,64,512]{3,1,2,0:T(8,128)} fusion(f32[1,48,64,512]{3,1,2,0:T(8,128)S(1)} %negate_bitcast_fusion, f32[1,48,64,512]{3,1,2,0:T(8,128)} %fusion.34), kind=kLoop, calls=%fused_computation.25 | loop fusion | flops 3145728 | bytes 25165824 | tf_op jit(solution)/shard_map/stack | solution.py:59
  550.3 16.4 %copy.24 = f32[2,48,64,512]{3,2,0,1:T(8,128)} copy(f32[2,48,64,512]{3,1,2,0:T(8,128)} %pad_maximum_fusion) | data formatting | bytes 25165824 | tf_op jit(solution)/shard_map/stack | solution.py:59
  566.7 278.0 %all_to_all.37 = f32[2,48,64,512]{3,2,0,1:T(8,128)} all-to-all(f32[2,48,64,512]{3,2,0,1:T(8,128)} %copy.24), channel_id=1, replica_groups=mesh['grp'=2,'blade'=8,'dof'=2] {'blade'}, dimensions={1} | all-to-all | bytes 25165824 | tf_op jit(solution)/shard_map/all_to_all | solution.py:60
  844.6 12.0 %copy.26 = f32[2,6,8,64,512]{4,3,2,1,0:T(8,128)} copy(f32[2,6,8,64,512]{4,3,0,1,2:T(8,128)} %bitcast.43) | data formatting | bytes 25165824 | tf_op jit(solution)/shard_map/all_to_all | solution.py:60
  856.6 20.9 %reduce-scatter.2.cloned.1.call-done = f32[2,6,256,512]{3,2,1,0:T(8,128)} async-done(((f32[2,6,512,512]{3,2,1,0:T(8,128)}), f32[2,6,256,512]{3,2,1,0:T(8,128)}) %reduce-scatter.2.cloned.1.call-update) | async-done | bytes 6291472 | tf_op jit(solution)/shard_map/reduce_scatter | solution.py:61
  (78 shorter events, 90.2 us)
Async XLA Ops:
  6.5 29.4 %copy-start = (bf16[256,512]{1,0:T(8,128)(2,1)S(1)}, bf16[256,512]{1,0:T(8,128)(2,1)}, u32[]{:S(2)}) copy-start(bf16[256,512]{1,0:T(8,128)(2,1)} %param.8) | copy-start | bytes 786436
  6.5 871.0 %reduce-scatter.2.cloned.1.call-start = ((), (), s32[]{:S(2)}) async-start(), calls=%async_computation.3 | async-start | bytes 18874368 | tf_op jit(solution)/shard_map/reduce_scatter | solution.py:61
  6.5 9.9 %collective-permute-start = (bf16[256,512]{1,0:T(8,128)(2,1)}, bf16[256,512]{1,0:T(8,128)(2,1)S(1)}, u32[]{:S(2)}, u32[]{:S(2)}) collective-permute-start(bf16[256,512]{1,0:T(8,128)(2,1)} %param.8), channel_id=1, source_target_pairs={{0,1},{1,2},{2,3},{3,4},{4,5},{5,6},{6,7},{7,8},{8,9},{9,10},{10,1... | collective-permute-start | bytes 786440 | tf_op jit(solution)/shard_map/ppermute | solution.py:17
  7.0 9.4 %collective-permute-start.1 = (bf16[256,512]{1,0:T(8,128)(2,1)}, bf16[256,512]{1,0:T(8,128)(2,1)S(1)}, u32[]{:S(2)}, u32[]{:S(2)}) collective-permute-start(bf16[256,512]{1,0:T(8,128)(2,1)} %param.8), channel_id=1, source_target_pairs={{0,15},{1,0},{2,1},{3,2},{4,3},{5,4},{6,5},{7,6},{8,7},{9,8},{10,9... | collective-permute-start | bytes 786440 | tf_op jit(solution)/shard_map/ppermute | solution.py:22
  16.4 8.6 collective-permute-start.2
  16.4 8.6 collective-permute-start.3
  25.0 8.6 collective-permute-start.4
  25.0 12.3 %collective-permute-start.5 = (bf16[256,512]{1,0:T(8,128)(2,1)S(1)}, bf16[256,512]{1,0:T(8,128)(2,1)S(1)}, u32[]{:S(2)}, u32[]{:S(2)}) collective-permute-start(bf16[256,512]{1,0:T(8,128)(2,1)S(1)} %collective-permute-done.3), channel_id=1, source_target_pairs={{0,15},{1,0},{2,1},{3,2},{4,3},{5,4},{6,5},{7,6},{8,7},{9,8},{10,9... | collective-permute-start | bytes 786440 | tf_op jit(solution)/shard_map/ppermute | solution.py:22
  33.6 8.9 %collective-permute-start.6 = (bf16[256,512]{1,0:T(8,128)(2,1)S(1)}, bf16[256,512]{1,0:T(8,128)(2,1)S(1)}, u32[]{:S(2)}, u32[]{:S(2)}) collective-permute-start(bf16[256,512]{1,0:T(8,128)(2,1)S(1)} %collective-permute-done.4), channel_id=1, source_target_pairs={{0,1},{1,2},{2,3},{3,4},{4,5},{5,6},{6,7},{7,8},{8,9},{9,10},{10,1... | collective-permute-start | bytes 786440 | tf_op jit(solution)/shard_map/ppermute | solution.py:17
  37.4 8.3 collective-permute-start.7
  42.5 8.6 collective-permute-start.8
  45.7 8.6 collective-permute-start.9
  51.1 8.6 collective-permute-start.10
  54.3 8.6 collective-permute-start.11
  59.7 8.6 collective-permute-start.12
  62.9 8.6 collective-permute-start.13
  68.3 8.5 collective-permute-start.14
Sparse Core Ops, SparseCore 0:
  856.7 20.7 reduce-scatter.1
